TPU v7x, 128 devices: a whole 4x4x4 slice. The times are simulated.
128 devices in a mesh: leaf: 16 (over y, z), ctx: 8 (over x, core).
Axes of the slice: x: 4, y: 4, z: 4, core: 2. Of those that a mesh axis runs over, the one named last changes fastest.
Arguments:
- query_key_value_rows: bfloat16 [16384, 7168], P(('leaf', 'ctx')), may hold values from -6 to 6
- cotangent: bfloat16 [16384, 5120], P(('leaf', 'ctx')), may hold values from -6 to 6
- out_weight: bfloat16 [5120, 5120], P('ctx'), may hold values from -0.078125 to 0.078125
- parents: int32 [16, 8], P('leaf'), may hold values from 0 to 6, as said below
- rollout_spans: int32 [16384], P('leaf'), may hold values from 64 to 4096
Outputs:
- qkv_grad: bfloat16 [16384, 7168], P(('leaf', 'ctx'))
- weight_grad: bfloat16 [5120, 5120], P('ctx')
Inputs may be any that keep to these rules, and one draw needn't show every extreme that they name: parents[t, 0] = 0, every later block's parent is an earlier block of the same tree, and the last block's parent is the block just before it.
All inputs are finite; a program needn't handle non-finite values.
Results may differ from a plain program's by a relative error of at most 0.012.
The roundings to bfloat16 on the way count: a program that leaves them out, or rounds other values in their place, can miss the bound.
Values may be sent and summed in bfloat16 or wider, within the bound.
No kernel may reach another device: no remote copies, remote signals or barrier semaphores. Data moves between devices by JAX's collectives and lax.ppermute only.
A program may use at most 192 MiB of HBM per device.

v0:
```python
import math
import jax
import jax.numpy as jnp
from jax import lax
from jax.sharding import PartitionSpec as P

QUERY_HEADS = 40
KEY_VALUE_HEADS = 8
HEAD_SIZE = 128
BLK = 128
log_base = 1024.0


def ancestors(parents):
    number = parents.shape[0]
    indices = jnp.arange(number, dtype=jnp.int32)

    def advance(iteration, state):
        current, reached = state
        current = jnp.sum(
            jnp.where(current[:, None] == indices[None, :], parents[None, :], 0), axis=1
        )
        return (current, reached | (current[:, None] == indices[None, :]))

    return lax.fori_loop(0, number, advance, (indices, indices[:, None] == indices[None, :]))[1]


def token_mask(reached, first_row, query_count, key_count):
    query_pos = first_row + jnp.arange(query_count, dtype=jnp.int32)
    key_pos = jnp.arange(key_count, dtype=jnp.int32)
    block_part = reached[first_row // BLK : (first_row + query_count) // BLK, : key_count // BLK]
    expanded = jnp.repeat(jnp.repeat(block_part, BLK, axis=0), BLK, axis=1)
    same_block = (query_pos // BLK)[:, None] == (key_pos // BLK)[None, :]
    return expanded & (jnp.logical_not(same_block) | (key_pos[None, :] <= query_pos[:, None]))


def span_softness(rollout_spans):
    return jnp.log(rollout_spans.astype(jnp.float32)) * (
        1.0 / (math.log(log_base) * math.sqrt(HEAD_SIZE))
    )


def contract_rows(left, right):
    return lax.dot_general(
        left, right, (((0,), (0,)), ((), ())), preferred_element_type=jnp.float32
    )


def contract_cols(left, right):
    return lax.dot_general(
        left, right, (((1,), (1,)), ((), ())), preferred_element_type=jnp.float32
    )


def local(query_key_value_rows, cotangent, out_weight, parents, rollout_spans):
    queries_per_group = QUERY_HEADS // KEY_VALUE_HEADS
    head_rows = lax.all_to_all(query_key_value_rows, "ctx", split_axis=1, concat_axis=0, tiled=True)
    tree_len = head_rows.shape[0]
    kv_local = head_rows.shape[1] // ((queries_per_group + 2) * HEAD_SIZE)
    heads_local = kv_local * queries_per_group
    grouped = head_rows.reshape(tree_len, kv_local, queries_per_group + 2, HEAD_SIZE)
    asking_matrix = grouped[:, :, :queries_per_group]
    lookup_matrix = grouped[:, :, queries_per_group]
    value_rows = grouped[:, :, queries_per_group + 1]
    softness_multiplier = span_softness(rollout_spans)
    reached = ancestors(parents[0])
    block_len = min(512, tree_len)
    block_total = tree_len // block_len
    masks = []
    total_parts = []
    attended_parts = []
    for block_id in range(block_total):
        opening_slot = block_id * block_len
        closing_slot = opening_slot + block_len
        allowed = token_mask(reached, opening_slot, block_len, closing_slot)
        masks.append(allowed)
        attention_logits = jnp.einsum(
            "zpyr,kpr->pyzk",
            asking_matrix[opening_slot:closing_slot],
            lookup_matrix[:closing_slot],
            preferred_element_type=jnp.float32,
        )
        attention_logits = jnp.where(
            allowed[None, None],
            attention_logits * softness_multiplier[opening_slot:closing_slot][None, None, :, None],
            -jnp.inf,
        )
        peak_score = jnp.max(attention_logits, axis=-1, keepdims=True)
        log_total = peak_score + jnp.log(
            jnp.sum(jnp.exp(attention_logits - peak_score), axis=-1, keepdims=True)
        )
        weights_low = jnp.exp(attention_logits - log_total).astype(jnp.bfloat16)
        attended_parts.append(
            jnp.einsum(
                "gjts,sgd->tgjd",
                weights_low,
                value_rows[:closing_slot],
                preferred_element_type=jnp.float32,
            ).astype(jnp.bfloat16)
        )
        total_parts.append(log_total[..., 0])
    attended = jnp.concatenate(attended_parts, axis=0)
    log_totals = jnp.concatenate(total_parts, axis=2)
    flat_out = attended.reshape(tree_len, heads_local * HEAD_SIZE)
    shard_rows = lax.all_gather(cotangent, "ctx", axis=0, tiled=True)
    weight_acc = contract_rows(flat_out, shard_rows)
    local_grad = contract_cols(shard_rows, out_weight).astype(jnp.bfloat16)
    weight_acc, output_gradient = (weight_acc, local_grad)
    weight_total = lax.psum(weight_acc, "leaf").astype(jnp.bfloat16)
    key_acc = jnp.zeros((tree_len, kv_local, HEAD_SIZE), jnp.float32)
    value_acc = jnp.zeros((tree_len, kv_local, HEAD_SIZE), jnp.float32)
    query_parts = []
    for head_id in range(heads_local):
        kv_id = head_id // queries_per_group
        inner = head_id % queries_per_group
        query_blocks = []
        for block_id in range(block_total):
            opening_slot = block_id * block_len
            closing_slot = opening_slot + block_len
            query_now = asking_matrix[opening_slot:closing_slot, kv_id, inner]
            keys_now = lookup_matrix[:closing_slot, kv_id]
            values_now = value_rows[:closing_slot, kv_id]
            line_multiplier = softness_multiplier[opening_slot:closing_slot][:, None]
            attention_logits = jnp.where(
                masks[block_id], contract_cols(query_now, keys_now) * line_multiplier, -jnp.inf
            )
            attention_probabilities = jnp.exp(
                attention_logits - log_totals[kv_id, inner, opening_slot:closing_slot][:, None]
            )
            grad_rows = output_gradient[
                opening_slot:closing_slot, head_id * HEAD_SIZE : (head_id + 1) * HEAD_SIZE
            ]
            own_rows = attended[opening_slot:closing_slot, kv_id, inner]
            probability_cotangent = contract_cols(grad_rows, values_now)
            middle_point = jnp.sum(
                grad_rows.astype(jnp.float32) * own_rows.astype(jnp.float32), axis=1
            )
            logit_cotangent = (
                attention_probabilities
                * (probability_cotangent - middle_point[:, None])
                * line_multiplier
            ).astype(jnp.bfloat16)
            query_blocks.append(
                jnp.dot(logit_cotangent, keys_now, preferred_element_type=jnp.float32).astype(
                    jnp.bfloat16
                )
            )
            key_acc = key_acc.at[:closing_slot, kv_id].add(
                contract_rows(logit_cotangent, query_now)
            )
            value_acc = value_acc.at[:closing_slot, kv_id].add(
                contract_rows(attention_probabilities.astype(jnp.bfloat16), grad_rows)
            )
        query_parts.append(jnp.concatenate(query_blocks, axis=0))
    query_grad = jnp.stack(query_parts, axis=1).reshape(
        tree_len, kv_local, queries_per_group, HEAD_SIZE
    )
    gradients = jnp.concatenate(
        [
            query_grad,
            key_acc.astype(jnp.bfloat16)[:, :, None],
            value_acc.astype(jnp.bfloat16)[:, :, None],
        ],
        axis=2,
    )
    gradients = gradients.reshape(tree_len, kv_local * (queries_per_group + 2) * HEAD_SIZE)
    returned = lax.all_to_all(gradients, "ctx", split_axis=0, concat_axis=1, tiled=True)
    return (returned, weight_total)


def solution(mesh):
    placed = (
        P(("leaf", "ctx"), None),
        P(("leaf", "ctx"), None),
        P("ctx", None),
        P("leaf", None),
        P("leaf"),
    )
    return jax.shard_map(
        local,
        mesh=mesh,
        in_specs=placed,
        out_specs=(P(("leaf", "ctx"), None), P("ctx", None)),
        check_vma=False,
    )
```

profile of v0, /device:TPU:0, one launch (start us, length us, event | category | flops | bytes accessed | tf_op | source)
XLA Modules:
  0.0 449.4 jit_solution(9614831033946304401)
XLA Ops:
  7.2 0.7 all-gather.2.cloned.1.call-update
  7.9 3.9 copy.35
  11.8 4.5 %all-to-all-start = ((bf16[128,8,896]{0,2,1:T(8,128)(2,1)}), bf16[128,8,896]{0,2,1:T(8,128)(2,1)S(1)}, u32[]{:S(2)}, u32[]{:S(2)}) async-start(bf16[128,8,896]{0,2,1:T(8,128)(2,1)} %bitcast.482), calls=%async_computation | async-start | bytes 3670016 | tf_op jit(solution)/shard_map/all_to_all | solution.py:57
  16.3 2.2 while.34
  18.6 1.6 broadcast_in_dim.71
  20.6 0.4 copy.38
  21.0 1.6 broadcast_in_dim.76
  22.6 0.8 fusion.14
  23.5 1.0 copy.42
  24.5 30.3 %all-to-all-done = bf16[128,8,896]{0,2,1:T(8,128)(2,1)S(1)} async-done(((bf16[128,8,896]{0,2,1:T(8,128)(2,1)}), bf16[128,8,896]{0,2,1:T(8,128)(2,1)S(1)}, u32[]{:S(2)}, u32[]{:S(2)}) %all-to-all-start) | async-done | bytes 1835040 | tf_op jit(solution)/shard_map/all_to_all | solution.py:57
  54.8 2.4 copy.36
  57.2 3.0 reshape.966
  60.3 1.0 fusion.8
  61.3 1.1 exponential_reduce_fusion.1
  62.4 1.8 fusion.3
  64.3 2.2 exponential_reduce_fusion
  66.5 1.6 fusion.54
  68.1 3.6 fusion.51
  71.7 1.3 pad_maximum_fusion.1
  73.0 1.4 fusion.37
  74.4 1.4 fusion.33
  75.9 1.5 fusion.35
  77.3 1.4 fusion.31
  78.7 2.4 fusion.39
  81.1 2.0 subtract_exponential_fusion.1
  83.1 2.1 subtract_exponential_fusion.3
  85.2 2.1 subtract_exponential_fusion.2
  87.3 2.0 subtract_exponential_fusion.4
  89.3 2.0 subtract_exponential_fusion
  91.3 11.9 %convolution_convert_fusion = bf16[1024,640]{0,1:T(8,128)(2,1)S(1)} fusion(bf16[1024,5120]{1,0:T(8,128)(2,1)} %all-gather.2.cloned.1.call-done, bf16[640,5120]{1,0:T(8,128)(2,1)} %param.49), kind=kOutput, calls=%fused_computation.35 | convolution fusion | flops 6711541760 | bytes 18350080 | tf_op jit(solution)/shard_map/dot_general | solution.py:50
  103.6 1.1 copy-done.4
  104.8 0.5 multiply_convert_fusion.4
  105.3 0.4 convolution_convert_fusion.10
  105.7 0.5 fusion.149
  110.8 14.2 %fusion.218 = f32[640,5120]{1,0:T(8,128)} fusion(bf16[1024,640]{0,1:T(8,128)(2,1)S(1)} %bitcast.489, bf16[1024,5120]{1,0:T(8,128)(2,1)} %all-gather.2.cloned.1.call-done), kind=kOutput, calls=%fused_computation.328 | convolution fusion | flops 6710886400 | bytes 24903680 | tf_op jit(solution)/shard_map/dot_general | solution.py:44
  125.0 0.5 multiply_convert_fusion.1
  125.5 0.4 convolution_convert_fusion.7
  126.0 0.6 copy-done.3
  126.6 0.5 multiply_convert_fusion.3
  127.1 0.4 convolution_convert_fusion.9
  127.5 0.6 copy-done.2
  128.2 0.5 multiply_convert_fusion.2
  128.7 0.4 convolution_convert_fusion.8
  129.1 0.5 fusion.61
  130.0 0.5 fusion.62
  130.9 0.5 fusion.63
  131.8 0.5 fusion.64
  133.4 0.5 fusion.57
  133.9 0.4 fusion.73
  134.3 0.5 fusion.58
  134.7 0.4 fusion.75
  135.1 0.5 fusion.59
  135.6 0.4 fusion.77
  136.0 0.7 copy-done
  136.7 0.5 fusion.71
  137.2 0.5 multiply_convert_fusion
  137.7 0.4 convolution_convert_fusion.6
  138.2 0.5 fusion.70
  139.1 2.5 copy.45
  141.6 2.0 copy.56
  143.7 1.5 copy.46
  145.2 3.6 all-to-all-start.1
  148.8 290.7 %all-reduce.2 = bf16[640,5120]{1,0:T(8,128)(2,1)} all-reduce(f32[640,5120]{1,0:T(8,128)} %fusion.218), channel_id=1, replica_groups=mesh['leaf'=16,'ctx'=8] {'leaf'}, use_global_device_ids=true, to_apply=%region_17.18 | all-reduce | flops 3276800 | bytes 19660800 | tf_op jit(solution)/shard_map/psum | solution.py:109
  439.5 2.9 copy.47
  (99 shorter events, 10.3 us)
Async XLA Ops:
  7.2 84.1 %all-gather.2.cloned.1.call-start = ((), (), s32[]{:S(2)}) async-start(), calls=%async_computation.2 | async-start | bytes 11796480 | tf_op jit(solution)/shard_map/all_gather | solution.py:105
  11.8 4.5 %copy-start.16 = (s32[1,8]{1,0:T(1,128)S(1)}, s32[1,8]{1,0:T(1,128)}, u32[]{:S(2)}) copy-start(s32[1,8]{1,0:T(1,128)} %param.50) | copy-start | bytes 100
  11.8 43.0 %all-to-all-start = ((bf16[128,8,896]{0,2,1:T(8,128)(2,1)}), bf16[128,8,896]{0,2,1:T(8,128)(2,1)S(1)}, u32[]{:S(2)}, u32[]{:S(2)}) async-start(bf16[128,8,896]{0,2,1:T(8,128)(2,1)} %bitcast.482), calls=%async_computation | async-start | bytes 3670016 | tf_op jit(solution)/shard_map/all_to_all | solution.py:57
  20.2 4.3 copy-start.15
  20.5 55.3 %copy-start.14 = (pred[512,512]{1,0:T(32,128)(4,1)}, pred[512,512]{1,0:T(32,128)(4,1)S(1)}, u32[]{:S(2)}) copy-start(pred[512,512]{1,0:T(32,128)(4,1)S(1)} %fusion.92) | copy-start | bytes 786436
  68.1 3.6 copy-start.11
  71.7 2.7 copy-start.9
  91.3 11.9 %copy-start.12 = (bf16[512,1,5,128]{0,3,2,1:T(8,128)(2,1)S(1)}, bf16[512,1,5,128]{0,3,2,1:T(8,128)(2,1)}, u32[]{:S(2)}) copy-start(bf16[512,1,5,128]{0,3,2,1:T(8,128)(2,1)} %copy-done.11) | copy-start | bytes 1966084
  91.3 12.1 %copy-start.10 = (bf16[512,1,5,128]{0,3,2,1:T(8,128)(2,1)S(1)}, bf16[512,1,5,128]{0,3,2,1:T(8,128)(2,1)}, u32[]{:S(2)}) copy-start(bf16[512,1,5,128]{0,3,2,1:T(8,128)(2,1)} %copy-done.9) | copy-start | bytes 1966084
  103.2 1.6 copy-start.4
  105.3 1.2 copy-start.5
  105.7 1.4 copy-start.8
  106.8 1.3 copy-start.7
  108.7 1.2 copy-start.6
  109.4 1.4 copy-start.13
  110.8 14.2 %copy-start.1 = (f32[512,1024]{1,0:T(8,128)S(1)}, f32[512,1024]{1,0:T(8,128)}, u32[]{:S(2)}) copy-start(f32[512,1024]{1,0:T(8,128)} %subtract_exponential_fusion.1) | copy-start | bytes 6291460
  125.0 1.6 copy-start.3
  126.6 1.6 copy-start.2
  135.1 1.6 copy-start
  145.2 294.3 %all-to-all-start.1 = ((bf16[8,128,896]{1,2,0:T(8,128)(2,1)}), bf16[8,128,896]{1,2,0:T(8,128)(2,1)S(1)}, u32[]{:S(2)}, u32[]{:S(2)}) async-start(bf16[8,128,896]{1,2,0:T(8,128)(2,1)} %copy.46), calls=%async_computation.1 | async-start | bytes 3670016 | tf_op jit(solution)/shard_map/all_to_all | solution.py:167
Sparse Core Ops, SparseCore 0:
  9.7 74.7 all-gather.1
where the time goes:
time: 454 us; the launch traced here: 449 us
  blocking collectives  291 us (64%)
  matrix products  68.7 us (15%)
  waiting for transfers between devices  31 us (7%)
  local copies, waits for them, and re-layouts  27.2 us (6%)
  between operations  14.9 us (3%)
  other arithmetic  8.79 us (2%)
  starting transfers between devices  8.15 us (2%)
    psum x1, blocking collectives, local(): weight_total = lax.psum(weight_acc, 'leaf').astype(jnp.bfloat16)  291 us
    dot_general x21, matrix products, contract_cols(): lax.dot_general(left, right, (((1,), (1,)), ((), ())), preferred_element_...  34.3 us
    all_to_all x1, waiting for transfers between devices, local(): lax.all_to_all(query_key_value_rows, 'ctx', split_axis=1, concat_axis=0,...  30.3 us
    dot_general x21, matrix products, contract_rows(): lax.dot_general(left, right, (((0,), (0,)), ((), ())), preferred_element_...  22.7 us
    unnamed x38, local copies, waits for them, and re-layouts  13 us
  transfers between devices with their start and end apart: 3, of which 1 were waited for; matrix products, arithmetic and copies ran while one was open for 11% of the time, Pallas kernels for 0%

commit v1 on v0

--- a/solution.py
+++ b/solution.py
@@ -9,6 +9,29 @@
 HEAD_SIZE = 128
 BLK = 128
 log_base = 1024.0
+
+
+def cut_along(shard, dim, devices):
+    shape = shard.shape
+    blocks = shard.reshape(*shape[:dim], devices, shape[dim] // devices, *shape[dim + 1 :])
+    return jnp.moveaxis(blocks, dim, 0)
+
+
+def laid_out(blocks, dim):
+    shape = list(blocks.shape[1:])
+    shape[dim] *= blocks.shape[0]
+    return jnp.moveaxis(blocks, 0, dim).reshape(shape)
+
+
+def pairwise_exchange(value, axis, split_dim, concat_dim):
+    devices, here = (lax.axis_size(axis), lax.axis_index(axis))
+    blocks = cut_along(value, split_dim, devices)
+    done = [blocks[here]]
+    for step in range(1, devices):
+        sent = blocks[here ^ step]
+        done.append(lax.ppermute(sent, axis, [(i, i ^ step) for i in range(devices)]))
+    blocks = jnp.stack(done)[here ^ jnp.arange(devices)]
+    return laid_out(blocks, concat_dim)
 
 
 def ancestors(parents):
@@ -54,7 +77,7 @@
 
 def local(query_key_value_rows, cotangent, out_weight, parents, rollout_spans):
     queries_per_group = QUERY_HEADS // KEY_VALUE_HEADS
-    head_rows = lax.all_to_all(query_key_value_rows, "ctx", split_axis=1, concat_axis=0, tiled=True)
+    head_rows = pairwise_exchange(query_key_value_rows, "ctx", 1, 0)
     tree_len = head_rows.shape[0]
     kv_local = head_rows.shape[1] // ((queries_per_group + 2) * HEAD_SIZE)
     heads_local = kv_local * queries_per_group

time: 454 us -> 499 us (1.099)
  local copies, waits for them, and re-layouts: 27.2 us -> 68.6 us
  waiting for transfers between devices: 31 us -> 23.7 us
  matrix products: 68.7 us -> 73.8 us
    all_to_all x1 -> x0, waiting for transfers between devices: 30.3 us -> none  [local(): lax.all_to_all(query_key_value_rows, 'ctx', split_axis=1, concat_axis=0,...]
    unnamed x38 -> x105, local copies, waits for them, and re-layouts: 13 us -> 40.5 us
    ppermute x0 -> x7, waiting for transfers between devices: none -> 23 us  [pairwise_exchange(): lax.ppermute(sent, axis, [(i, i ^ step) for i in range(devices)])]
    dot_general x2, matrix products: 5.18 us -> 16.5 us  [local(): jnp.einsum('gjts,sgd->tgjd', weights_low, value_rows[:closing_slot], pref...]
    another operation x0 -> x11, local copies, waits for them, and re-layouts: none -> 10.4 us
    ppermute x0 -> x7, starting transfers between devices: none -> 8.23 us  [pairwise_exchange(): lax.ppermute(sent, axis, [(i, i ^ step) for i in range(devices)])]
    slice x0 -> x3, local copies, waits for them, and re-layouts: none -> 5.75 us  [the longest x1 3.69 us: local(): values_now = value_rows[:closing_slot, kv_id]]
  transfers between devices with their start and end apart: 3 -> 9, of which waited for: 1 -> 4; matrix products, arithmetic and copies ran while one was open for 11% -> 20% of each run, Pallas kernels for 0% -> 0%
where the time goes in v1:
time: 499 us; the launch traced here: 492 us
  blocking collectives  290 us (58%)
  matrix products  73.8 us (15%)
  local copies, waits for them, and re-layouts  68.6 us (14%)
  waiting for transfers between devices  23.7 us (5%)
  between operations  15.4 us (3%)
  starting transfers between devices  11.9 us (2%)
  other arithmetic  8.72 us (2%)
    psum x1, blocking collectives, local(): weight_total = lax.psum(weight_acc, 'leaf').astype(jnp.bfloat16)  290 us
    unnamed x105, local copies, waits for them, and re-layouts  40.5 us
    dot_general x21, matrix products, contract_cols(): lax.dot_general(left, right, (((1,), (1,)), ((), ())), preferred_element_...  31.8 us
    ppermute x7, waiting for transfers between devices, pairwise_exchange(): lax.ppermute(sent, axis, [(i, i ^ step) for i in range(devices)])  23 us
    dot_general x21, matrix products, contract_rows(): lax.dot_general(left, right, (((0,), (0,)), ((), ())), preferred_element_...  18.5 us
    dot_general x2, matrix products, local(): jnp.einsum('gjts,sgd->tgjd', weights_low, value_rows[:closing_slot], pref...  16.5 us
  transfers between devices with their start and end apart: 9, of which 4 were waited for; matrix products, arithmetic and copies ran while one was open for 20% of the time, Pallas kernels for 0%

profile of v1, /device:TPU:0, one launch (start us, length us, event | category | flops | bytes accessed | tf_op | source)
XLA Modules:
  0.0 492.4 jit_solution(16354595102000033225)
XLA Ops:
  7.9 3.3 copy.44
  12.1 0.9 copy.46
  13.8 1.6 collective-permute-start.1
  17.4 3.1 collective-permute-start.3
  20.5 0.9 copy.50
  21.4 2.2 while.34
  23.9 1.6 broadcast_in_dim.71
  25.9 1.6 broadcast_in_dim.76
  28.3 1.0 copy.55
  29.4 1.6 copy.59
  31.0 1.1 copy.52
  32.2 2.9 collective-permute-start.5
  35.2 1.0 bitcast_dynamic-update-slice_fusion.7
  36.5 1.0 bitcast_dynamic-update-slice_fusion.6
  37.4 1.0 bitcast_dynamic-update-slice_fusion.5
  38.4 3.7 collective-permute-done.3
  42.1 1.0 bitcast_dynamic-update-slice_fusion.4
  43.1 7.3 %collective-permute-done.4 = bf16[128,896]{1,0:T(8,128)(2,1)} collective-permute-done((bf16[128,896]{1,0:T(8,128)(2,1)}, bf16[128,896]{1,0:T(8,128)(2,1)}, u32[]{:S(2)}, u32[]{:S(2)}) %collective-permute-start.4) | collective-permute-done | bytes 229408 | tf_op jit(solution)/shard_map/ppermute | solution.py:32
  50.4 1.0 bitcast_dynamic-update-slice_fusion.3
  51.4 2.5 collective-permute-done.5
  53.9 9.5 %collective-permute-done.6 = bf16[128,896]{1,0:T(8,128)(2,1)S(1)} collective-permute-done((bf16[128,896]{1,0:T(8,128)(2,1)S(1)}, bf16[128,896]{1,0:T(8,128)(2,1)S(1)}, u32[]{:S(2)}, u32[]{:S(2)}) %collective-permute-start.6) | collective-permute-done | bytes 229408 | tf_op jit(solution)/shard_map/ppermute | solution.py:32
  63.5 2.0 gather_fusion
  65.4 3.9 reshape.1042
  69.4 1.9 fusion.203
  71.3 1.2 copy.79
  72.5 1.1 copy.77
  73.6 3.7 fusion.202
  77.3 1.7 copy.75
  79.1 1.0 copy.73
  80.0 1.7 copy.85
  81.8 1.7 copy.84
  83.5 1.7 copy.83
  85.2 1.7 copy.82
  87.0 1.7 copy.81
  88.7 1.7 copy.80
  90.5 1.7 copy.76
  92.2 1.8 copy.72
  93.9 1.7 copy.87
  95.7 1.8 copy.86
  98.4 1.0 fusion.8
  99.4 1.1 exponential_reduce_fusion.1
  100.5 2.3 fusion.3
  102.8 2.2 exponential_reduce_fusion
  105.0 1.6 fusion.54
  106.7 14.9 %fusion.51 = bf16[512,1,5,128]{0,3,2,1:T(8,128)(2,1)S(1)} fusion(f32[1024,512,5]{1,0,2:T(8,128)S(1)} %get-tuple-element.356, f32[5,512]{1,0:T(8,128)S(1)} %log_add_fusion, f32[512]{0:T(512)S(1)} %get-tuple-element.354, pred[512,1024]{0,1:T(8,128)(4,1)S(1)} %copy-done.11, bf16[1024,1,1,128]{0,3,2,1:T(8,128)(2,1)S(1)} %copy.79), kind=kOutput, calls=%fused_computation.80 | convolution fusion | flops 681902080 | bytes 11939840 | tf_op jit(solution)/shard_map/gjts,sgd->tgjd/dot_general | solution.py:117
  121.6 1.2 pad_maximum_fusion.1
  122.9 1.4 fusion.37
  124.3 1.4 fusion.35
  125.7 1.4 fusion.33
  127.2 1.4 fusion.31
  128.6 1.4 fusion.39
  130.0 2.0 subtract_exponential_fusion.1
  132.0 2.0 subtract_exponential_fusion.2
  134.1 2.1 subtract_exponential_fusion.3
  136.1 2.0 subtract_exponential_fusion.4
  138.9 11.8 %convolution_convert_fusion = bf16[1024,640]{0,1:T(8,128)(2,1)S(1)} fusion(bf16[1024,5120]{1,0:T(8,128)(2,1)} %all-gather.2.cloned.1.call-done, bf16[640,5120]{1,0:T(8,128)(2,1)} %param.49), kind=kOutput, calls=%fused_computation.36 | convolution fusion | flops 6711541760 | bytes 18350080 | tf_op jit(solution)/shard_map/dot_general | solution.py:73
  151.2 1.1 copy-done.3
  158.4 10.1 %fusion.208 = f32[640,5120]{1,0:T(8,128)} fusion(bf16[1024,640]{0,1:T(8,128)(2,1)S(1)} %bitcast.492, bf16[1024,5120]{1,0:T(8,128)(2,1)S(1)} %copy-done.38), kind=kOutput, calls=%fused_computation.327 | convolution fusion | flops 6710886400 | bytes 24903680 | tf_op jit(solution)/shard_map/dot_general | solution.py:67
  182.4 2.5 copy.62
  185.0 2.0 copy.90
  187.0 1.5 copy.63
  188.5 3.6 all-to-all-start
  192.1 290.1 %all-reduce.2 = bf16[640,5120]{1,0:T(8,128)(2,1)} all-reduce(f32[640,5120]{1,0:T(8,128)} %fusion.208), channel_id=1, replica_groups=mesh['leaf'=16,'ctx'=8] {'leaf'}, use_global_device_ids=true, to_apply=%region_17.18 | all-reduce | flops 3276800 | bytes 19660800 | tf_op jit(solution)/shard_map/psum | solution.py:132
  482.3 2.9 copy.64
  (193 shorter events, 30.4 us)
Async XLA Ops:
  7.2 131.7 %all-gather.2.cloned.1.call-start = ((), (), s32[]{:S(2)}) async-start(), calls=%async_computation.1 | async-start | bytes 11796480 | tf_op jit(solution)/shard_map/all_gather | solution.py:128
  11.3 10.1 %copy-start.39 = (s32[1,8]{1,0:T(1,128)S(1)}, s32[1,8]{1,0:T(1,128)}, u32[]{:S(2)}) copy-start(s32[1,8]{1,0:T(1,128)} %param.50) | copy-start | bytes 100
  12.1 11.7 %copy-start.37 = (s32[1024]{0:T(1024)S(1)}, s32[1024]{0:T(1024)}, u32[]{:S(2)}) copy-start(s32[1024]{0:T(1024)} %param.51) | copy-start | bytes 12292
  13.0 19.3 %collective-permute-start = (bf16[128,896]{1,0:T(8,128)(2,1)}, bf16[128,896]{1,0:T(8,128)(2,1)}, u32[]{:S(2)}, u32[]{:S(2)}) collective-permute-start(bf16[128,896]{1,0:T(8,128)(2,1)} %bitcast.3), channel_id=1, source_target_pairs={{0,1},{1,0},{2,3},{3,2},{4,5},{5,4},{6,7},{7,6},{8,9},{9,8},{10,11... | collective-permute-start | bytes 688136 | tf_op jit(solution)/shard_map/ppermute | solution.py:32
  13.8 22.3 %collective-permute-start.1 = (bf16[128,896]{1,0:T(8,128)(2,1)}, bf16[128,896]{1,0:T(8,128)(2,1)}, u32[]{:S(2)}, u32[]{:S(2)}) collective-permute-start(bf16[128,896]{1,0:T(8,128)(2,1)} %bitcast.5), channel_id=1, source_target_pairs={{0,2},{1,3},{2,0},{3,1},{4,6},{5,7},{6,4},{7,5},{8,10},{9,11},{10,... | collective-permute-start | bytes 688136 | tf_op jit(solution)/shard_map/ppermute | solution.py:32
  16.2 21.2 %collective-permute-start.2 = (bf16[128,896]{1,0:T(8,128)(2,1)}, bf16[128,896]{1,0:T(8,128)(2,1)}, u32[]{:S(2)}, u32[]{:S(2)}) collective-permute-start(bf16[128,896]{1,0:T(8,128)(2,1)} %bitcast.7), channel_id=1, source_target_pairs={{0,3},{1,2},{2,1},{3,0},{4,7},{5,6},{6,5},{7,4},{8,11},{9,10},{10,... | collective-permute-start | bytes 688136 | tf_op jit(solution)/shard_map/ppermute | solution.py:32
  17.4 24.8 %collective-permute-start.3 = (bf16[128,896]{1,0:T(8,128)(2,1)}, bf16[128,896]{1,0:T(8,128)(2,1)}, u32[]{:S(2)}, u32[]{:S(2)}) collective-permute-start(bf16[128,896]{1,0:T(8,128)(2,1)} %bitcast.9), channel_id=1, source_target_pairs={{0,4},{1,5},{2,6},{3,7},{4,0},{5,1},{6,2},{7,3},{8,12},{9,13},{10,... | collective-permute-start | bytes 688136 | tf_op jit(solution)/shard_map/ppermute | solution.py:32
  21.3 29.1 %collective-permute-start.4 = (bf16[128,896]{1,0:T(8,128)(2,1)}, bf16[128,896]{1,0:T(8,128)(2,1)}, u32[]{:S(2)}, u32[]{:S(2)}) collective-permute-start(bf16[128,896]{1,0:T(8,128)(2,1)} %bitcast.11), channel_id=1, source_target_pairs={{0,5},{1,4},{2,7},{3,6},{4,1},{5,0},{6,3},{7,2},{8,13},{9,12},{10,... | collective-permute-start | bytes 688136 | tf_op jit(solution)/shard_map/ppermute | solution.py:32
  32.2 21.6 %collective-permute-start.5 = (bf16[128,896]{1,0:T(8,128)(2,1)S(1)}, bf16[128,896]{1,0:T(8,128)(2,1)S(1)}, u32[]{:S(2)}, u32[]{:S(2)}) collective-permute-start(bf16[128,896]{1,0:T(8,128)(2,1)S(1)} %bitcast.497), channel_id=1, source_target_pairs={{0,6},{1,7},{2,4},{3,5},{4,2},{5,3},{6,0},{7,1},{8,14},{9,15},{10,... | collective-permute-start | bytes 688136 | tf_op jit(solution)/shard_map/ppermute | solution.py:32
  36.1 27.3 %collective-permute-start.6 = (bf16[128,896]{1,0:T(8,128)(2,1)S(1)}, bf16[128,896]{1,0:T(8,128)(2,1)S(1)}, u32[]{:S(2)}, u32[]{:S(2)}) collective-permute-start(bf16[128,896]{1,0:T(8,128)(2,1)S(1)} %bitcast.496), channel_id=1, source_target_pairs={{0,7},{1,6},{2,5},{3,4},{4,3},{5,2},{6,1},{7,0},{8,15},{9,14},{10,... | collective-permute-start | bytes 688136 | tf_op jit(solution)/shard_map/ppermute | solution.py:32
  97.4 0.9 copy-start.16
  99.4 1.1 copy-start.11
  102.8 2.2 copy-start.9
  106.7 14.9 %copy-start.14 = (bf16[512,1,5,128]{0,3,2,1:T(8,128)(2,1)}, bf16[512,1,5,128]{0,3,2,1:T(8,128)(2,1)S(1)}, u32[]{:S(2)}) copy-start(bf16[512,1,5,128]{0,3,2,1:T(8,128)(2,1)S(1)} %fusion.54) | copy-start | bytes 1966084
  121.6 2.7 copy-start.12
  121.6 1.3 copy-start.20
  121.6 2.7 copy-start.26
  122.8 2.9 copy-start.29
  122.9 4.3 copy-start.31
  124.3 4.3 copy-start.24
  125.7 4.3 copy-start.18
  128.6 3.4 copy-start.22
  132.0 2.0 copy-start.28
  134.1 2.1 copy-start.33
  136.1 2.0 copy-start.35
  138.9 12.1 %copy-start.13 = (bf16[512,1,5,128]{0,3,2,1:T(8,128)(2,1)S(1)}, bf16[512,1,5,128]{0,3,2,1:T(8,128)(2,1)}, u32[]{:S(2)}) copy-start(bf16[512,1,5,128]{0,3,2,1:T(8,128)(2,1)} %copy-done.12) | copy-start | bytes 1966084
  138.9 11.8 %copy-start.15 = (bf16[512,1,5,128]{0,3,2,1:T(8,128)(2,1)S(1)}, bf16[512,1,5,128]{0,3,2,1:T(8,128)(2,1)}, u32[]{:S(2)}) copy-start(bf16[512,1,5,128]{0,3,2,1:T(8,128)(2,1)} %copy-done.14) | copy-start | bytes 1966084
  138.9 19.3 %copy-start.38 = (bf16[1024,5120]{1,0:T(8,128)(2,1)S(1)}, bf16[1024,5120]{1,0:T(8,128)(2,1)}, u32[]{:S(2)}) copy-start(bf16[1024,5120]{1,0:T(8,128)(2,1)} %all-gather.2.cloned.1.call-done) | copy-start | bytes 31457284
  150.7 1.6 copy-start.3
  152.3 1.0 copy-start.34
  152.8 1.2 copy-start.4
  152.8 1.2 copy-start.10
  153.3 1.4 copy-start.6
  154.4 1.3 copy-start.7
  155.1 1.3 copy-start.8
  156.4 1.2 copy-start.5
  157.0 1.3 copy-start.17
  158.4 10.1 %copy-start = (f32[512,1024]{1,0:T(8,128)S(1)}, f32[512,1024]{1,0:T(8,128)}, u32[]{:S(2)}) copy-start(f32[512,1024]{1,0:T(8,128)} %subtract_exponential_fusion.1) | copy-start | bytes 6291460
  168.5 1.6 copy-start.1
  170.1 1.6 copy-start.2
  175.7 0.9 copy-start.32
  175.7 1.3 copy-start.30
  176.6 1.2 copy-start.27
  177.0 1.3 copy-start.23
  177.8 0.9 copy-start.21
  177.8 1.3 copy-start.19
  178.8 0.9 copy-start.25
  180.6 0.9 copy-start.36
  188.5 293.7 %all-to-all-start = ((bf16[8,128,896]{1,2,0:T(8,128)(2,1)}), bf16[8,128,896]{1,2,0:T(8,128)(2,1)S(1)}, u32[]{:S(2)}, u32[]{:S(2)}) async-start(bf16[8,128,896]{1,2,0:T(8,128)(2,1)} %copy.63), calls=%async_computation | async-start | bytes 3670016 | tf_op jit(solution)/shard_map/all_to_all | solution.py:190
Sparse Core Ops, SparseCore 0:
  9.7 80.6 all-gather.1
